TPU v7x, 256 devices: a whole 4x4x8 slice. The times are simulated.
256 devices in a mesh: seq: 32 (over x_hi, z, core), tensor: 8 (over y, x_lo).
Axes of the slice: x: 4 (x_hi: 2, x_lo: 2; x = x_hi * 2 + x_lo), y: 4, z: 8, core: 2. Of those that a mesh axis runs over, the one named last changes fastest.
Arguments:
- tokens: bfloat16 [4, 1024, 4096], P(None, 'seq', 'tensor'), may hold values from -600 to 600
- norm_gain: bfloat16 [4096], replicated, may hold values from 0.099609375 to 1.8984375
- w_query: bfloat16 [4096, 2048], P(None, 'tensor'), may hold values from -0.1875 to 0.1875
- w_key: bfloat16 [4096, 2048], P(None, 'tensor'), may hold values from -0.09375 to 0.09375
- w_value: bfloat16 [4096, 2048], P(None, 'tensor'), may hold values from -0.09375 to 0.09375
- w_out: bfloat16 [2048, 4096], P('tensor'), may hold values from -1 to 1
- cache_keys: bfloat16 [4, 8192, 2048], P(None, 'seq', 'tensor'), may hold values from -103 to 103
- cache_values: bfloat16 [4, 8192, 2048], P(None, 'seq', 'tensor'), may hold values from -6 to 6
- cache_len: int32 [4], replicated, may hold values from 1 to 8192, as said below
- group_len: int32 [4], replicated, may hold values from 1 to 1024, 3584 in all
Outputs:
- mixed: bfloat16 [4, 1024, 4096], P(None, 'seq', 'tensor')
- new_keys: bfloat16 [4, 1024, 2048], P(None, 'seq', 'tensor')
- new_values: bfloat16 [4, 1024, 2048], P(None, 'seq', 'tensor')
Inputs may be any that keep to these rules, and one draw needn't show every extreme that they name: `cache_len`: one request's cache holds all 8192 positions. `group_len`: the new-token counts sum to 3584.
All inputs are finite; a program needn't handle non-finite values.
Results may differ from a plain program's by a relative error of at most 0.0075.
The roundings to bfloat16 on the way count: a program that leaves them out, or rounds other values in their place, can miss the bound.
Values may be sent and summed in bfloat16 or wider, within the bound.
No kernel may reach another device: no remote copies, remote signals or barrier semaphores. Data moves between devices by JAX's collectives and lax.ppermute only.
A program may use at most 128 MiB of HBM per device.

v0:
```python
import jax
import jax.numpy as jnp
from jax import lax
from jax.sharding import PartitionSpec as P

HD = 128


def rotate(vector, position):
    half_dim = vector.shape[-1] // 2
    frequency = 1000000.0 ** (-(jnp.arange(half_dim, dtype=jnp.float32) * 2.0 / vector.shape[-1]))
    angles = position.astype(jnp.float32)[..., None] * frequency
    cosine = jnp.concatenate([jnp.cos(angles), jnp.cos(angles)], -1)[..., None, :]
    sine = jnp.concatenate([jnp.sin(angles), jnp.sin(angles)], -1)[..., None, :]
    turned = jnp.concatenate([-vector[..., half_dim:], vector[..., :half_dim]], -1)
    return vector * cosine + turned * sine


def body(
    tokens,
    norm_gain,
    w_query,
    w_key,
    w_value,
    w_out,
    cache_keys,
    cache_values,
    cache_len,
    group_len,
):
    seq_index = lax.axis_index("seq")
    requests, local_rows, width_part = tokens.shape
    gathered = lax.all_gather(tokens, "tensor", axis=2, tiled=True).astype(jnp.float32)
    inverse_rms = lax.rsqrt(jnp.mean(gathered * gathered, -1, keepdims=True) + 1e-05)
    normed = (gathered * inverse_rms * norm_gain.astype(jnp.float32)).astype(jnp.bfloat16)
    flat_rows = normed.reshape(requests * local_rows, -1)
    heads_width = w_query.shape[1]
    local_heads = heads_width // HD

    def project(weight):
        return jnp.dot(flat_rows, weight, preferred_element_type=jnp.float32).reshape(
            requests, local_rows, local_heads, HD
        )

    offsets = jnp.arange(local_rows, dtype=jnp.int32)
    first_row = seq_index * local_rows
    position = cache_len[:, None] + first_row + offsets[None, :]
    queries = (
        rotate(project(w_query), position)
        .astype(jnp.bfloat16)
        .reshape(requests, local_rows, heads_width)
    )
    key_new = (
        rotate(project(w_key), position)
        .astype(jnp.bfloat16)
        .reshape(requests, local_rows, heads_width)
    )
    value_new = project(w_value).astype(jnp.bfloat16).reshape(requests, local_rows, heads_width)
    live_rows = (first_row + offsets)[None, :] < group_len[:, None]
    new_keys = jnp.where(live_rows[..., None], key_new, jnp.zeros_like(key_new))
    new_values = jnp.where(live_rows[..., None], value_new, jnp.zeros_like(value_new))
    all_queries = lax.all_gather(queries, "seq", axis=1, tiled=True)
    group_total = all_queries.shape[1]
    cache_slots = cache_keys.shape[1]
    block_keys = cache_slots + local_rows
    slot_index = seq_index * cache_slots + jnp.arange(cache_slots, dtype=jnp.int32)
    query_index = jnp.arange(group_total, dtype=jnp.int32)
    token_index = first_row + offsets
    score_scale = HD ** (-0.5)
    numer_list = []
    peak_list = []
    mass_list = []
    for request in range(requests):
        query_rows = all_queries[request].reshape(group_total, local_heads, HD)
        key_rows = jnp.concatenate([cache_keys[request], key_new[request]], 0).reshape(
            block_keys, local_heads, HD
        )
        value_rows = jnp.concatenate([cache_values[request], value_new[request]], 0).reshape(
            block_keys, local_heads, HD
        )
        scores = (
            jnp.einsum("qhd,khd->hqk", query_rows, key_rows, preferred_element_type=jnp.float32)
            * score_scale
        )
        cache_ok = slot_index < cache_len[request]
        group_ok = (token_index[None, :] <= query_index[:, None]) & (
            token_index < group_len[request]
        )[None, :]
        usable = jnp.concatenate(
            [jnp.broadcast_to(cache_ok[None, :], (group_total, cache_slots)), group_ok], 1
        )[None]
        row_peak = jnp.max(jnp.where(usable, scores, -1e30), -1)
        weights = jnp.where(usable, jnp.exp(scores - row_peak[..., None]), 0.0)
        row_mass = jnp.sum(weights, -1)
        numer_list.append(
            jnp.einsum(
                "hqk,khd->qhd",
                weights.astype(jnp.bfloat16),
                value_rows,
                preferred_element_type=jnp.float32,
            )
        )
        peak_list.append(row_peak.T)
        mass_list.append(row_mass.T)
    numerators = jnp.stack(numer_list)
    row_peaks = jnp.stack(peak_list)
    row_masses = jnp.stack(mass_list)
    top_peak = lax.pmax(row_peaks.astype(jnp.bfloat16), "seq").astype(row_peaks.dtype)
    factor = jnp.exp(row_peaks - top_peak)
    scaled = (numerators * factor[..., None]).reshape(requests, group_total, heads_width)
    numer_sum, mass_sum = (
        lax.psum_scatter(scaled, "seq", scatter_dimension=1, tiled=True),
        lax.psum_scatter(row_masses * factor, "seq", scatter_dimension=1, tiled=True),
    )
    attended = numer_sum.reshape(requests, local_rows, local_heads, HD) / mass_sum[..., None]
    attended = (
        jnp.where(live_rows[..., None, None], attended, 0.0)
        .astype(jnp.bfloat16)
        .reshape(requests * local_rows, heads_width)
    )
    partial_out = jnp.dot(attended, w_out, preferred_element_type=jnp.float32).reshape(
        requests, local_rows, -1
    )
    mixed = lax.psum_scatter(partial_out, "tensor", scatter_dimension=2, tiled=True).astype(
        jnp.bfloat16
    )
    return (mixed, new_keys, new_values)


def solution(mesh):
    placed = (
        P(None, "seq", "tensor"),
        P(),
        P(None, "tensor"),
        P(None, "tensor"),
        P(None, "tensor"),
        P("tensor", None),
        P(None, "seq", "tensor"),
        P(None, "seq", "tensor"),
        P(),
        P(),
    )
    return jax.shard_map(
        body,
        mesh=mesh,
        in_specs=placed,
        out_specs=(P(None, "seq", "tensor"), P(None, "seq", "tensor"), P(None, "seq", "tensor")),
        check_vma=False,
    )
```

profile of v0, /device:TPU:32, one launch (start us, length us, event | category | flops | bytes accessed | tf_op | source)
XLA Modules:
  0.0 642.3 jit_solution(6151474447986249479)
XLA Ops:
  7.2 0.7 all-gather.3.cloned.1.call-update
  8.0 0.7 convert_element_type.53
  8.7 4.1 copy.101
  12.8 4.1 copy.100
  17.4 38.2 %all-gather.3.cloned.1.call-done = bf16[4,32,4096]{2,1,0:T(8,128)(2,1)} async-done(((bf16[4,32,512]{2,1,0:T(8,128)(2,1)}), bf16[4,32,4096]{2,1,0:T(8,128)(2,1)}) %all-gather.3.cloned.1.call-update) | async-done | bytes 1048592 | tf_op jit(solution)/shard_map/all_gather | solution.py:33
  55.6 1.7 fusion
  57.3 2.8 fusion.77
  60.1 0.8 fusion.79
  62.2 0.7 fusion.106
  63.1 4.1 copy.99
  67.2 0.7 fusion.105
  67.9 1.0 copy.105
  68.9 0.8 copy.60
  70.4 1.2 fusion.84
  71.6 1.0 copy.108
  72.6 0.7 copy.72
  73.4 1.0 copy.107
  74.4 0.8 copy.69
  75.1 1.2 fusion.82
  76.5 0.7 copy.78
  77.4 0.7 copy.75
  78.2 0.8 copy.84
  79.1 0.8 copy.81
  80.5 1.3 broadcast_compare_fusion.1
  81.9 1.4 broadcast_compare_fusion.3
  83.5 0.9 pad_add_fusion.1
  84.4 0.9 pad_add_fusion.2
  86.0 2.8 convolution_convert_fusion
  89.5 50.7 %all-gather.5.cloned.1.call-done = bf16[4,1024,256]{2,1,0:T(8,128)(2,1)} async-done(((bf16[4,32,256]{2,1,0:T(8,128)(2,1)}), bf16[4,1024,256]{2,1,0:T(8,128)(2,1)}) %all-gather.5.cloned.1.call-update) | async-done | bytes 2097168 | tf_op jit(solution)/shard_map/all_gather | solution.py:62
  140.1 2.8 fusion.104
  143.0 1.2 copy.63
  144.9 1.2 fusion.5
  146.0 1.8 fusion.19
  147.9 1.6 copy.86
  149.4 2.1 copy.70
  151.5 1.8 select_reduce_fusion.2
  153.3 1.2 fusion.7
  154.5 1.8 fusion.17
  156.3 2.5 copy.87
  158.8 2.0 copy.76
  160.9 1.9 select_reduce_fusion.1
  162.8 1.2 fusion.9
  163.9 1.8 fusion.15
  165.7 2.6 copy.88
  168.3 2.0 copy.82
  170.4 3.2 select_reduce_fusion
  174.2 125.7 %pmax.7 = bf16[4,1024,2]{1,2,0:T(2,128)(2,1)S(1)} all-reduce(bf16[4,1024,2]{1,2,0:T(2,128)(2,1)} %fusion.103), channel_id=1, replica_groups=mesh['seq'=32,'tensor'=8] {'seq'}, use_global_device_ids=true, to_apply=%region_5.6 | all-reduce | flops 8192 | bytes 32768 | tf_op jit(solution)/shard_map/pmax | solution.py:108
  300.0 2.3 fusion.11
  302.3 0.7 maximum_multiply_fusion.3
  302.9 2.7 copy.90
  305.7 7.0 %mul.122 = f32[4,1024,2,128]{3,2,1,0:T(2,128)} broadcast(f32[4,1024,2]{2,1,0:T(8,128)} %copy.90), dimensions={0,1,2} | broadcast | bytes 4227072 | tf_op jit(solution)/shard_map/mul | solution.py:110
  312.7 6.4 mul.123
  319.1 3.6 fusion.13
  322.7 2.5 copy.89
  325.2 2.4 copy.102
  327.7 3.0 reshape.250
  330.8 5.6 maximum_multiply_fusion
  337.1 109.7 %reduce-scatter.10.cloned.1.call-done = f32[32,8]{1,0:T(8,128)} async-done(((f32[1024,8]{1,0:T(8,128)}), f32[32,8]{1,0:T(8,128)}) %reduce-scatter.10.cloned.1.call-update) | async-done | bytes 1040
  446.9 0.8 reshape.251
  448.0 129.2 %reduce-scatter.6.cloned.1.call-done = f32[4,32,256]{2,1,0:T(8,128)} async-done(((f32[4,1024,256]{2,1,0:T(8,128)}), f32[4,32,256]{2,1,0:T(8,128)}) %reduce-scatter.6.cloned.1.call-update) | async-done | bytes 131088 | tf_op jit(solution)/shard_map/reduce_scatter | solution.py:112
  577.2 2.7 fusion.3
  580.0 0.7 bitcast_select_fusion
  580.7 53.5 %reduce-scatter.8.cloned.1.call-done = f32[4,32,512]{2,1,0:T(8,128)} async-done(((f32[4,32,4096]{2,1,0:T(8,128)}), f32[4,32,512]{2,1,0:T(8,128)}) %reduce-scatter.8.cloned.1.call-update) | async-done | bytes 262160 | tf_op jit(solution)/shard_map/reduce_scatter | solution.py:124
  634.2 1.6 convert_element_type.66
  (92 shorter events, 7.8 us)
Async XLA Ops:
  7.2 570.0 %copy-start = (bf16[256,4096]{1,0:T(8,128)(2,1)S(1)}, bf16[256,4096]{1,0:T(8,128)(2,1)}, u32[]{:S(2)}) copy-start(bf16[256,4096]{1,0:T(8,128)(2,1)} %param.15) | copy-start | bytes 6291460
  7.2 48.4 %all-gather.3.cloned.1.call-start = ((), (), s32[]{:S(2)}) async-start(), calls=%async_computation.3 | async-start | bytes 1179648 | tf_op jit(solution)/shard_map/all_gather | solution.py:33
  7.9 132.2 %all-gather.5.cloned.1.call-start = ((), (), s32[]{:S(2)}) async-start(), calls=%async_computation.4 | async-start | bytes 2162688 | tf_op jit(solution)/shard_map/all_gather | solution.py:62
  12.7 4.2 copy-start.18
  55.6 4.5 copy-start.3
  55.6 4.5 copy-start.4
  57.3 3.7 copy-start.21
  60.1 2.1 copy-start.5
  61.9 385.0 %reduce-scatter.10.cloned.1.call-start = ((), (), s32[]{:S(2)}) async-start(), calls=%async_computation.7 | async-start | bytes 540672
  62.9 4.3 copy-start.6
  67.2 12.7 %copy-start.19 = (s32[4]{0:T(128)S(1)}, s32[4]{0:T(128)}, u32[]{:S(2)}) copy-start(s32[4]{0:T(128)} %param.19) | copy-start | bytes 52
  71.6 14.5 %copy-start.22 = (f32[4,32]{1,0:T(4,128)S(1)}, f32[4,32]{1,0:T(4,128)}, u32[]{:S(2)}) copy-start(f32[4,32]{1,0:T(4,128)} %copy-done.21) | copy-start | bytes 1540
  79.9 9.0 %copy-start.23 = (s32[32]{0:T(128)}, s32[32]{0:T(128)S(1)}, u32[]{:S(2)}) copy-start(s32[32]{0:T(128)S(1)} %iota_add_fusion.1) | copy-start | bytes 388
  88.8 55.4 %copy-start.7 = (bf16[4,32,2,128]{3,1,2,0:T(8,128)(2,1)}, bf16[4,32,2,128]{3,1,2,0:T(8,128)(2,1)S(1)}, u32[]{:S(2)}) copy-start(bf16[4,32,2,128]{3,1,2,0:T(8,128)(2,1)S(1)} %convolution_convert_fusion) | copy-start | bytes 196612
  144.2 1.8 copy-start.9
  151.5 1.9 copy-start.2
  151.5 3.0 copy-start.10
  151.5 3.0 copy-start.17
  160.9 1.9 copy-start.1
  160.9 3.0 copy-start.11
  160.9 3.0 copy-start.16
  300.0 2.3 copy-start.12
  300.0 2.3 copy-start.13
  300.0 2.3 copy-start.14
  312.7 6.4 copy-start.15
  330.7 246.5 %reduce-scatter.6.cloned.1.call-start = ((), (), s32[]{:S(2)}) async-start(), calls=%async_computation.5 | async-start | bytes 4325376 | tf_op jit(solution)/shard_map/reduce_scatter | solution.py:112
  336.4 0.7 copy-start.20
  336.4 0.7 copy-start.24
  336.4 297.7 %reduce-scatter.8.cloned.1.call-start = ((), (), s32[]{:S(2)}) async-start(), calls=%async_computation.6 | async-start | bytes 2359296 | tf_op jit(solution)/shard_map/reduce_scatter | solution.py:124
  448.0 131.9 %copy-start.8 = (bf16[4,32,2,128]{3,1,2,0:T(8,128)(2,1)S(1)}, bf16[4,32,2,128]{3,1,2,0:T(8,128)(2,1)}, u32[]{:S(2)}) copy-start(bf16[4,32,2,128]{3,1,2,0:T(8,128)(2,1)} %copy-done.7) | copy-start | bytes 196612
Sparse Core Ops, SparseCore 0:
  9.8 45.7 all-gather.2
  62.0 78.0 all-gather.4
  330.9 115.9 reduce-scatter.9
  451.0 126.1 reduce-scatter.5
  580.1 54.0 reduce-scatter.7
where the time goes:
time: 645 us; the launch traced here: 642 us
  waiting for transfers between devices  382 us (59%)
  blocking collectives  126 us (20%)
  local copies, waits for them, and re-layouts  68.8 us (11%)
  matrix products  25.7 us (4%)
  other arithmetic  25.6 us (4%)
  between operations  14.2 us (2%)
    reduce_scatter x1, waiting for transfers between devices, body(): lax.psum_scatter(scaled, 'seq', scatter_dimension=1, tiled=True)  129 us
    pmax x1, blocking collectives, body(): lax.pmax(row_peaks.astype(jnp.bfloat16), 'seq').astype(row_peaks.dtype)  126 us
    unnamed x6, waiting for transfers between devices  110 us
    reduce_scatter x1, waiting for transfers between devices, body(): lax.psum_scatter(partial_out, 'tensor', scatter_dimension=2, tiled=True)  53.5 us
    all_gather x1, waiting for transfers between devices, body(): all_queries = lax.all_gather(queries, 'seq', axis=1, tiled=True)  50.7 us
    all_gather x1, waiting for transfers between devices, body(): lax.all_gather(tokens, 'tensor', axis=2, tiled=True).astype(jnp.float32)  38.2 us
    mul x2, local copies, waits for them, and re-layouts, body(): numerators * factor[..., None]  13.4 us
  transfers between devices with their start and end apart: 5, of which 5 were waited for; matrix products, arithmetic and copies ran while one was open for 7% of the time, Pallas kernels for 0%

commit v1 on v0

--- a/solution.py
+++ b/solution.py
@@ -105,7 +105,9 @@
     numerators = jnp.stack(numer_list)
     row_peaks = jnp.stack(peak_list)
     row_masses = jnp.stack(mass_list)
-    top_peak = lax.pmax(row_peaks.astype(jnp.bfloat16), "seq").astype(row_peaks.dtype)
+    seq_count = group_total // local_rows
+    all_peaks = lax.all_gather(row_peaks.astype(jnp.bfloat16), "seq", axis=0)
+    top_peak = jnp.max(all_peaks, 0).astype(row_peaks.dtype)
     factor = jnp.exp(row_peaks - top_peak)
     scaled = (numerators * factor[..., None]).reshape(requests, group_total, heads_width)
     numer_sum, mass_sum = (

time: 645 us -> 561 us (0.87)
  blocking collectives: 126 us -> 41.9 us
    pmax x1 -> x0, blocking collectives: 126 us -> none  [body(): lax.pmax(row_peaks.astype(jnp.bfloat16), 'seq').astype(row_peaks.dtype)]
    all_gather x0 -> x1, blocking collectives: none -> 41.9 us  [body(): all_peaks = lax.all_gather(row_peaks.astype(jnp.bfloat16), 'seq', axis=0)]
  transfers between devices with their start and end apart: 5 -> 5, of which waited for: 5 -> 5; matrix products, arithmetic and copies ran while one was open for 7% -> 8% of each run, Pallas kernels for 0% -> 0%
where the time goes in v1:
time: 561 us; the launch traced here: 558 us
  waiting for transfers between devices  377 us (67%)
  local copies, waits for them, and re-layouts  72.4 us (13%)
  blocking collectives  41.9 us (7%)
  other arithmetic  27.9 us (5%)
  matrix products  24.3 us (4%)
  between operations  14.2 us (3%)
    reduce_scatter x1, waiting for transfers between devices, body(): lax.psum_scatter(scaled, 'seq', scatter_dimension=1, tiled=True)  129 us
    unnamed x6, waiting for transfers between devices  106 us
    reduce_scatter x1, waiting for transfers between devices, body(): lax.psum_scatter(partial_out, 'tensor', scatter_dimension=2, tiled=True)  53.4 us
    all_gather x1, waiting for transfers between devices, body(): all_queries = lax.all_gather(queries, 'seq', axis=1, tiled=True)  50.7 us
    all_gather x1, blocking collectives, body(): all_peaks = lax.all_gather(row_peaks.astype(jnp.bfloat16), 'seq', axis=0)  41.9 us
    all_gather x1, waiting for transfers between devices, body(): lax.all_gather(tokens, 'tensor', axis=2, tiled=True).astype(jnp.float32)  38.2 us
    mul x2, local copies, waits for them, and re-layouts, body(): numerators * factor[..., None]  13.4 us
    dot_general x3, local copies, waits for them, and re-layouts, project(): jnp.dot(flat_rows, weight, preferred_element_type=jnp.float32)  12.3 us
  transfers between devices with their start and end apart: 5, of which 5 were waited for; matrix products, arithmetic and copies ran while one was open for 8% of the time, Pallas kernels for 0%

profile of v1, /device:TPU:32, one launch (start us, length us, event | category | flops | bytes accessed | tf_op | source)
XLA Modules:
  0.0 558.4 jit_solution(6900690896149172971)
XLA Ops:
  8.0 0.7 convert_element_type.62
  8.7 4.1 copy.181
  12.8 4.1 copy.180
  17.4 38.2 %all-gather.3.cloned.1.call-done = bf16[4,32,4096]{2,1,0:T(8,128)(2,1)} async-done(((bf16[4,32,512]{2,1,0:T(8,128)(2,1)}), bf16[4,32,4096]{2,1,0:T(8,128)(2,1)}) %all-gather.3.cloned.1.call-update) | async-done | bytes 1048592 | tf_op jit(solution)/shard_map/all_gather | solution.py:33
  55.6 1.7 fusion
  57.3 2.8 fusion.77
  60.1 0.8 fusion.79
  62.2 0.7 fusion.109
  63.1 4.1 copy.179
  67.2 0.7 fusion.108
  68.0 1.0 copy.186
  69.0 0.8 copy.136
  70.4 1.3 fusion.87
  71.7 1.0 copy.189
  72.7 0.8 copy.148
  73.5 1.0 copy.188
  74.5 0.8 copy.145
  75.2 1.2 fusion.85
  76.5 0.7 copy.154
  77.4 0.8 copy.151
  78.3 0.8 copy.160
  79.1 0.8 copy.157
  80.6 1.3 broadcast_compare_fusion.1
  81.9 1.3 broadcast_compare_fusion.3
  83.5 0.9 pad_add_fusion.1
  84.4 0.9 pad_add_fusion.2
  86.0 2.8 convolution_convert_fusion
  89.4 50.7 %all-gather.5.cloned.1.call-done = bf16[4,1024,256]{2,1,0:T(8,128)(2,1)} async-done(((bf16[4,32,256]{2,1,0:T(8,128)(2,1)}), bf16[4,1024,256]{2,1,0:T(8,128)(2,1)}) %all-gather.5.cloned.1.call-update) | async-done | bytes 2097168 | tf_op jit(solution)/shard_map/all_gather | solution.py:62
  140.1 2.9 fusion.107
  143.0 1.2 copy.139
  145.5 1.2 fusion.5
  146.7 1.8 fusion.19
  148.5 1.6 copy.162
  150.0 2.1 copy.146
  152.1 1.8 select_reduce_fusion.2
  154.6 1.2 fusion.7
  155.7 1.8 fusion.17
  157.5 2.5 copy.163
  160.1 2.1 copy.152
  162.1 1.9 select_reduce_fusion.1
  164.6 1.2 fusion.9
  165.7 1.8 fusion.15
  167.6 2.6 copy.164
  170.1 2.1 copy.158
  172.2 1.8 select_reduce_fusion
  174.0 0.8 pad_maximum_fusion.2
  174.8 41.9 %all_gather.12 = bf16[32,4,1024,2]{2,1,3,0:T(4,128)(2,1)} all-gather(bf16[1,4,1024,2]{2,1,3,0:T(4,128)(2,1)S(1)} %copy.168), channel_id=1, replica_groups=mesh['seq'=32,'tensor'=8] {'seq'}, dimensions={0}, use_global_device_ids=true | all-gather | bytes 540672 | tf_op jit(solution)/shard_map/all_gather | solution.py:109
  220.9 1.3 reduce_max.49
  222.2 1.5 maximum_multiply_fusion.3
  223.7 2.7 copy.169
  226.4 7.0 %mul.122 = f32[4,1024,2,128]{3,2,1,0:T(2,128)} broadcast(f32[4,1024,2]{2,1,0:T(8,128)} %copy.169), dimensions={0,1,2} | broadcast | bytes 4227072 | tf_op jit(solution)/shard_map/mul | solution.py:112
  233.4 6.4 %mul.123 = f32[4,1024,256]{2,1,0:T(8,128)} reshape(f32[4,1024,2,128]{3,2,1,0:T(2,128)} %mul.122) | data formatting | bytes 8388608 | tf_op jit(solution)/shard_map/mul | solution.py:112
  239.8 3.6 fusion.13
  243.4 2.5 copy.165
  246.0 2.5 copy.182
  248.4 3.1 reshape.349
  251.5 5.6 %maximum_multiply_fusion = f32[4,1024,256]{2,1,0:T(8,128)} fusion(f32[4,1024,256]{2,1,0:T(8,128)} %mul.123, f32[1,1024,256]{2,1,0:T(8,128)} %copy.165, f32[1,1024,256]{2,1,0:T(8,128)} %copy.164, f32[1,1024,256]{2,1,0:T(8,128)} %copy.163, f32[1,1024,256]{2,1,0:T(8,128)S(1)} %copy.162), kind=kLoop, calls=%fused_computation | loop fusion | flops 4194304 | bytes 12582912 | tf_op jit(solution)/shard_map/mul | solution.py:112
  257.9 105.1 %reduce-scatter.10.cloned.1.call-done = f32[32,8]{1,0:T(8,128)} async-done(((f32[1024,8]{1,0:T(8,128)}), f32[32,8]{1,0:T(8,128)}) %reduce-scatter.10.cloned.1.call-update) | async-done | bytes 1040
  363.0 0.8 reshape.350
  364.2 129.2 %reduce-scatter.6.cloned.1.call-done = f32[4,32,256]{2,1,0:T(8,128)} async-done(((f32[4,1024,256]{2,1,0:T(8,128)}), f32[4,32,256]{2,1,0:T(8,128)}) %reduce-scatter.6.cloned.1.call-update) | async-done | bytes 131088 | tf_op jit(solution)/shard_map/reduce_scatter | solution.py:114
  493.3 2.7 fusion.3
  496.1 0.7 bitcast_select_fusion
  496.9 53.4 %reduce-scatter.8.cloned.1.call-done = f32[4,32,512]{2,1,0:T(8,128)} async-done(((f32[4,32,4096]{2,1,0:T(8,128)}), f32[4,32,512]{2,1,0:T(8,128)}) %reduce-scatter.8.cloned.1.call-update) | async-done | bytes 262160 | tf_op jit(solution)/shard_map/reduce_scatter | solution.py:126
  550.2 1.6 convert_element_type.74
  (110 shorter events, 13.9 us)
Async XLA Ops:
  7.2 486.2 %copy-start = (bf16[256,4096]{1,0:T(8,128)(2,1)S(1)}, bf16[256,4096]{1,0:T(8,128)(2,1)}, u32[]{:S(2)}) copy-start(bf16[256,4096]{1,0:T(8,128)(2,1)} %param.15) | copy-start | bytes 6291460
  7.2 48.4 %all-gather.3.cloned.1.call-start = ((), (), s32[]{:S(2)}) async-start(), calls=%async_computation.3 | async-start | bytes 1179648 | tf_op jit(solution)/shard_map/all_gather | solution.py:33
  7.9 132.2 %all-gather.5.cloned.1.call-start = ((), (), s32[]{:S(2)}) async-start(), calls=%async_computation.4 | async-start | bytes 2162688 | tf_op jit(solution)/shard_map/all_gather | solution.py:62
  12.8 4.1 copy-start.20
  55.6 4.5 copy-start.4
  55.6 4.5 copy-start.5
  57.3 3.7 copy-start.23
  60.1 2.1 copy-start.6
  61.9 301.1 %reduce-scatter.10.cloned.1.call-start = ((), (), s32[]{:S(2)}) async-start(), calls=%async_computation.7 | async-start | bytes 540672
  62.9 4.4 copy-start.7
  67.2 12.7 %copy-start.21 = (s32[4]{0:T(128)S(1)}, s32[4]{0:T(128)}, u32[]{:S(2)}) copy-start(s32[4]{0:T(128)} %param.19) | copy-start | bytes 52
  71.7 14.3 %copy-start.24 = (f32[4,32]{1,0:T(4,128)S(1)}, f32[4,32]{1,0:T(4,128)}, u32[]{:S(2)}) copy-start(f32[4,32]{1,0:T(4,128)} %copy-done.23) | copy-start | bytes 1540
  79.9 8.9 %copy-start.25 = (s32[32]{0:T(128)}, s32[32]{0:T(128)S(1)}, u32[]{:S(2)}) copy-start(s32[32]{0:T(128)S(1)} %iota_add_fusion.1) | copy-start | bytes 388
  88.8 55.4 %copy-start.8 = (bf16[4,32,2,128]{3,1,2,0:T(8,128)(2,1)}, bf16[4,32,2,128]{3,1,2,0:T(8,128)(2,1)S(1)}, u32[]{:S(2)}) copy-start(bf16[4,32,2,128]{3,1,2,0:T(8,128)(2,1)S(1)} %convolution_convert_fusion) | copy-start | bytes 196612
  144.3 2.4 copy-start.10
  152.1 2.5 copy-start.3
  152.1 3.6 copy-start.12
  152.1 3.6 copy-start.19
  162.1 2.5 copy-start.2
  162.1 3.6 copy-start.11
  162.1 3.6 copy-start.18
  172.2 44.5 %copy-start.13 = (f32[2,1024]{1,0:T(2,128)S(1)}, f32[2,1024]{1,0:T(2,128)}, u32[]{:S(2)}) copy-start(f32[2,1024]{1,0:T(2,128)} %fusion.5) | copy-start | bytes 24580
  172.2 44.5 %copy-start.14 = (f32[2,1024]{1,0:T(2,128)S(1)}, f32[2,1024]{1,0:T(2,128)}, u32[]{:S(2)}) copy-start(f32[2,1024]{1,0:T(2,128)} %fusion.7) | copy-start | bytes 24580
  172.2 45.7 %copy-start.15 = (f32[2,1024]{1,0:T(2,128)S(1)}, f32[2,1024]{1,0:T(2,128)}, u32[]{:S(2)}) copy-start(f32[2,1024]{1,0:T(2,128)} %fusion.9) | copy-start | bytes 24580
  174.0 45.2 %copy-start.1 = (f32[2,1024,288]{1,2,0:T(8,128)}, f32[2,1024,288]{1,2,0:T(8,128)S(1)}, u32[]{:S(2)}) copy-start(f32[2,1024,288]{1,2,0:T(8,128)S(1)} %get-tuple-element.48) | copy-start | bytes 7077892
  219.1 3.1 copy-start.16
  233.4 6.4 %copy-start.17 = (bf16[32,2,128]{2,0,1:T(8,128)(2,1)S(1)}, bf16[32,2,128]{2,0,1:T(8,128)(2,1)}, u32[]{:S(2)}) copy-start(bf16[32,2,128]{2,0,1:T(8,128)(2,1)} %get-tuple-element.24) | copy-start | bytes 49156
  251.5 241.8 %reduce-scatter.6.cloned.1.call-start = ((), (), s32[]{:S(2)}) async-start(), calls=%async_computation.5 | async-start | bytes 4325376 | tf_op jit(solution)/shard_map/reduce_scatter | solution.py:114
  257.2 0.7 copy-start.22
  257.2 0.7 copy-start.26
  257.2 293.0 %reduce-scatter.8.cloned.1.call-start = ((), (), s32[]{:S(2)}) async-start(), calls=%async_computation.6 | async-start | bytes 2359296 | tf_op jit(solution)/shard_map/reduce_scatter | solution.py:126
  364.2 131.9 %copy-start.9 = (bf16[4,32,2,128]{3,1,2,0:T(8,128)(2,1)S(1)}, bf16[4,32,2,128]{3,1,2,0:T(8,128)(2,1)}, u32[]{:S(2)}) copy-start(bf16[4,32,2,128]{3,1,2,0:T(8,128)(2,1)} %copy-done.8) | copy-start | bytes 196612
Sparse Core Ops, SparseCore 0:
  9.8 45.7 all-gather.2
  62.0 78.0 all-gather.4
  251.6 111.3 reduce-scatter.9
  367.1 126.1 reduce-scatter.5
  496.2 53.9 reduce-scatter.7

commit v2 on v1

--- a/solution.py
+++ b/solution.py
@@ -106,14 +106,31 @@
     row_peaks = jnp.stack(peak_list)
     row_masses = jnp.stack(mass_list)
     seq_count = group_total // local_rows
-    all_peaks = lax.all_gather(row_peaks.astype(jnp.bfloat16), "seq", axis=0)
-    top_peak = jnp.max(all_peaks, 0).astype(row_peaks.dtype)
-    factor = jnp.exp(row_peaks - top_peak)
-    scaled = (numerators * factor[..., None]).reshape(requests, group_total, heads_width)
-    numer_sum, mass_sum = (
-        lax.psum_scatter(scaled, "seq", scatter_dimension=1, tiled=True),
-        lax.psum_scatter(row_masses * factor, "seq", scatter_dimension=1, tiled=True),
+    numer_width = requests * local_rows * heads_width
+    numer_chunks = (
+        numerators.reshape(requests, seq_count, local_rows * heads_width)
+        .transpose(1, 0, 2)
+        .reshape(seq_count, numer_width)
     )
+    stats = (
+        jnp.stack([row_peaks, row_masses], -1)
+        .reshape(requests, seq_count, local_rows * local_heads * 2)
+        .transpose(1, 0, 2)
+        .reshape(seq_count, -1)
+    )
+    payload = jnp.concatenate([numer_chunks, stats], -1)
+    received = lax.all_to_all(payload, "seq", 0, 0, tiled=True)
+    block_numer = received[:, :numer_width].reshape(
+        seq_count, requests, local_rows, local_heads, HD
+    )
+    block_stats = received[:, numer_width:].reshape(
+        seq_count, requests, local_rows, local_heads, 2
+    )
+    block_peak = block_stats[..., 0]
+    top_peak = jnp.max(block_peak, 0)
+    factor = jnp.exp(block_peak - top_peak)
+    numer_sum = jnp.sum(block_numer * factor[..., None], 0)
+    mass_sum = jnp.sum(block_stats[..., 1] * factor, 0)
     attended = numer_sum.reshape(requests, local_rows, local_heads, HD) / mass_sum[..., None]
     attended = (
         jnp.where(live_rows[..., None, None], attended, 0.0)

time: 561 us -> 404 us (0.72)
  waiting for transfers between devices: 377 us -> 245 us
  blocking collectives: 41.9 us -> 0 us
  local copies, waits for them, and re-layouts: 72.4 us -> 81.9 us
    reduce_scatter x1 -> x0, waiting for transfers between devices: 129 us -> none  [body(): lax.psum_scatter(scaled, 'seq', scatter_dimension=1, tiled=True)]
    unnamed x6 -> x3, waiting for transfers between devices: 106 us -> 0.71 us
    all_to_all x0 -> x1, waiting for transfers between devices: none -> 96.5 us  [body(): received = lax.all_to_all(payload, 'seq', 0, 0, tiled=True)]
    all_gather x1 -> x0, blocking collectives: 41.9 us -> none  [body(): all_peaks = lax.all_gather(row_peaks.astype(jnp.bfloat16), 'seq', axis=0)]
    all_to_all x0 -> x2, local copies, waits for them, and re-layouts: none -> 23.3 us  [body(): received = lax.all_to_all(payload, 'seq', 0, 0, tiled=True)]
    mul x2 -> x0, local copies, waits for them, and re-layouts: 13.4 us -> none  [body(): numerators * factor[..., None]]
    reduce_sum x0 -> x2, other arithmetic: none -> 8.6 us  [the longest x1 8.21 us: body(): numer_sum = jnp.sum(block_numer * factor[..., None], 0)]
    transpose x0 -> x5, local copies, waits for them, and re-layouts: none -> 8.59 us  [the longest x4 6.38 us: body(): jnp.einsum('hqk,khd->qhd', weights.astype(jnp.bfloat16), value_rows, pref...]
  transfers between devices with their start and end apart: 5 -> 4, of which waited for: 5 -> 4; matrix products, arithmetic and copies ran while one was open for 8% -> 8% of each run, Pallas kernels for 0% -> 0%
where the time goes in v2:
time: 404 us; the launch traced here: 401 us
  waiting for transfers between devices  245 us (61%)
  local copies, waits for them, and re-layouts  81.9 us (20%)
  other arithmetic  28 us (7%)
  matrix products  25.9 us (6%)
  between operations  14.4 us (4%)
  starting transfers between devices  5.92 us (1%)
    all_to_all x1, waiting for transfers between devices, body(): received = lax.all_to_all(payload, 'seq', 0, 0, tiled=True)  96.5 us
    all_gather x1, waiting for transfers between devices, body(): all_queries = lax.all_gather(queries, 'seq', axis=1, tiled=True)  55.4 us
    reduce_scatter x1, waiting for transfers between devices, body(): lax.psum_scatter(partial_out, 'tensor', scatter_dimension=2, tiled=True)  54.4 us
    all_gather x1, waiting for transfers between devices, body(): lax.all_gather(tokens, 'tensor', axis=2, tiled=True).astype(jnp.float32)  38.1 us
    all_to_all x2, local copies, waits for them, and re-layouts, body(): received = lax.all_to_all(payload, 'seq', 0, 0, tiled=True)  23.3 us
    dot_general x4, matrix products, body(): jnp.einsum('hqk,khd->qhd', weights.astype(jnp.bfloat16), value_rows, pref...  14 us
    dot_general x3, local copies, waits for them, and re-layouts, project(): jnp.dot(flat_rows, weight, preferred_element_type=jnp.float32)  12.4 us
    slice x5, local copies, waits for them, and re-layouts, body(): query_rows = all_queries[request].reshape(group_total, local_heads, HD)  11.1 us
  transfers between devices with their start and end apart: 4, of which 4 were waited for; matrix products, arithmetic and copies ran while one was open for 8% of the time, Pallas kernels for 0%

profile of v2, /device:TPU:32, one launch (start us, length us, event | category | flops | bytes accessed | tf_op | source)
XLA Modules:
  0.0 401.2 jit_solution(9434015722190370377)
XLA Ops:
  7.2 0.7 all-gather.3.cloned.1.call-update
  8.0 0.7 convert_element_type.47
  8.7 4.1 %copy.149 = bf16[256,4096]{1,0:T(8,128)(2,1)} copy(bf16[256,4096]{0,1:T(8,128)(2,1)} %bitcast.144) | data formatting | bytes 4194304 | tf_op jit(solution)/shard_map/dot_general | solution.py:41
  12.8 4.1 %copy.150 = bf16[256,4096]{1,0:T(8,128)(2,1)} copy(bf16[256,4096]{0,1:T(8,128)(2,1)} %bitcast.145) | data formatting | bytes 4194304 | tf_op jit(solution)/shard_map/dot_general | solution.py:41
  17.5 38.1 %all-gather.3.cloned.1.call-done = bf16[4,32,4096]{2,1,0:T(8,128)(2,1)} async-done(((bf16[4,32,512]{2,1,0:T(8,128)(2,1)}), bf16[4,32,4096]{2,1,0:T(8,128)(2,1)}) %all-gather.3.cloned.1.call-update) | async-done | bytes 1048592 | tf_op jit(solution)/shard_map/all_gather | solution.py:33
  55.6 1.7 fusion.1
  57.3 2.8 fusion.76
  60.1 0.8 fusion.74
  61.3 0.6 copy.170
  61.9 0.7 fusion.104
  62.6 1.3 fusion.79
  63.9 1.2 fusion.81
  65.6 0.8 copy.124
  66.4 0.8 copy.117
  67.3 0.8 copy.131
  68.0 1.1 fusion.101
  69.3 0.8 copy.104
  70.1 0.8 copy.121
  71.0 0.8 copy.114
  71.9 0.8 copy.128
  72.6 4.1 %copy.148 = bf16[256,4096]{1,0:T(8,128)(2,1)} copy(bf16[256,4096]{0,1:T(8,128)(2,1)} %bitcast.146) | data formatting | bytes 4194304 | tf_op jit(solution)/shard_map/dot_general | solution.py:41
  76.8 0.6 fusion.105
  77.4 1.2 broadcast_compare_fusion.3
  78.7 1.2 broadcast_compare_fusion.1
  80.7 2.8 convolution_convert_fusion
  83.5 0.6 copy-done.16
  84.2 0.6 slice_bitcast_fusion.7
  84.8 55.4 %all-gather.5.cloned.1.call-done = bf16[4,1024,256]{2,1,0:T(8,128)(2,1)} async-done(((bf16[4,32,256]{2,1,0:T(8,128)(2,1)}), bf16[4,1024,256]{2,1,0:T(8,128)(2,1)}) %all-gather.5.cloned.1.call-update) | async-done | bytes 2097168 | tf_op jit(solution)/shard_map/all_gather | solution.py:62
  140.2 2.9 fusion.100
  143.1 2.0 copy.107
  145.1 2.0 copy.129
  147.2 2.1 copy.122
  149.2 2.1 copy.115
  151.3 1.8 select_reduce_fusion.2
  153.7 0.9 copy-done.3
  155.8 0.8 copy-done.2
  158.7 1.4 copy-done.4
  160.8 2.3 copy.135
  163.1 2.2 copy.136
  165.3 0.6 copy.169
  166.0 3.4 convolution_bitcast_fusion.2
  169.4 1.5 copy.119
  171.0 1.9 stack.55
  172.8 3.6 convolution_bitcast_fusion.1
  176.4 1.5 copy.126
  178.0 1.8 stack.56
  179.8 3.5 convolution_bitcast_fusion.3
  183.3 1.5 copy.112
  184.9 1.8 stack.54
  186.7 3.5 convolution_bitcast_fusion
  190.2 1.8 copy.133
  191.9 1.8 stack.57
  193.8 2.5 maximum_bitcast_fusion.1
  197.1 2.3 maximum_bitcast_fusion
  199.4 8.5 %copy.137 = f32[32,1,33280]{2,1,0:T(1,128)} copy(f32[32,1,33280]{2,0,1:T(8,128)} %maximum_bitcast_fusion) | data formatting | bytes 8519680 | tf_op jit(solution)/shard_map/all_to_all | solution.py:122
  207.9 5.8 %all-to-all-start = ((f32[32,1,33280]{2,1,0:T(1,128)}), f32[32,1,33280]{2,1,0:T(1,128)}, u32[]{:S(2)}, u32[]{:S(2)}) async-start(f32[32,1,33280]{2,1,0:T(1,128)} %copy.137), calls=%async_computation | async-start | bytes 8519680 | tf_op jit(solution)/shard_map/all_to_all | solution.py:122
  213.9 96.5 %all-to-all-done = f32[32,1,33280]{2,1,0:T(1,128)} async-done(((f32[32,1,33280]{2,1,0:T(1,128)}), f32[32,1,33280]{2,1,0:T(1,128)}, u32[]{:S(2)}, u32[]{:S(2)}) %all-to-all-start) | async-done | bytes 4259872 | tf_op jit(solution)/shard_map/all_to_all | solution.py:122
  310.4 14.8 %copy.138 = f32[32,1,33280]{0,2,1:T(8,128)} copy(f32[32,1,33280]{2,1,0:T(1,128)} %all-to-all-done) | data formatting | bytes 8519680 | tf_op jit(solution)/shard_map/all_to_all | solution.py:122
  325.1 1.0 slice.169
  327.1 8.2 %fusion = f32[32768]{0:T(1024)S(1)} fusion(f32[32,33280]{0,1:T(8,128)} %bitcast.137, f32[32,4,32,2]{0,3,2,1:T(2,128)S(1)} %bitcast.152), kind=kLoop, calls=%fused_computation.1 | loop fusion | flops 2064384 | bytes 4358144 | tf_op jit(solution)/shard_map/reduce_sum | solution.py:132
  336.1 1.8 fusion.4
  337.9 0.7 bitcast_select_fusion
  338.7 54.4 %reduce-scatter.2.cloned.1.call-done = f32[4,32,512]{2,1,0:T(8,128)} async-done(((f32[4,32,4096]{2,1,0:T(8,128)}), f32[4,32,512]{2,1,0:T(8,128)}) %reduce-scatter.2.cloned.1.call-update) | async-done | bytes 262160 | tf_op jit(solution)/shard_map/reduce_scatter | solution.py:143
  393.1 1.6 convert_element_type.58
  (108 shorter events, 9.8 us)
Async XLA Ops:
  7.2 328.9 %copy-start = (bf16[256,4096]{1,0:T(8,128)(2,1)S(1)}, bf16[256,4096]{1,0:T(8,128)(2,1)}, u32[]{:S(2)}) copy-start(bf16[256,4096]{1,0:T(8,128)(2,1)} %param.15) | copy-start | bytes 6291460
  7.2 48.4 %all-gather.3.cloned.1.call-start = ((), (), s32[]{:S(2)}) async-start(), calls=%async_computation.2 | async-start | bytes 1179648 | tf_op jit(solution)/shard_map/all_gather | solution.py:33
  7.9 132.3 %all-gather.5.cloned.1.call-start = ((), (), s32[]{:S(2)}) async-start(), calls=%async_computation.3 | async-start | bytes 2162688 | tf_op jit(solution)/shard_map/all_gather | solution.py:62
  8.7 51.4 %copy-start.19 = (f32[4096]{0:T(1024)}, f32[4096]{0:T(1024)S(1)}, u32[]{:S(2)}) copy-start(f32[4096]{0:T(1024)S(1)} %convert_element_type.47) | copy-start | bytes 49156
  12.8 4.1 %copy-start.24 = (s32[4]{0:T(128)S(1)}, s32[4]{0:T(128)}, u32[]{:S(2)}) copy-start(s32[4]{0:T(128)} %param.18) | copy-start | bytes 52
  55.6 4.5 %copy-start.10 = (bf16[256,4096]{1,0:T(8,128)(2,1)S(1)}, bf16[256,4096]{1,0:T(8,128)(2,1)}, u32[]{:S(2)}) copy-start(bf16[256,4096]{1,0:T(8,128)(2,1)} %copy.150) | copy-start | bytes 6291460
  55.6 4.5 %copy-start.11 = (bf16[4,32,4096]{2,1,0:T(8,128)(2,1)S(1)}, bf16[4,32,4096]{2,1,0:T(8,128)(2,1)}, u32[]{:S(2)}) copy-start(bf16[4,32,4096]{2,1,0:T(8,128)(2,1)} %all-gather.3.cloned.1.call-done) | copy-start | bytes 3145732
  57.3 2.8 copy-start.27
  60.1 5.1 %copy-start.14 = (bf16[4,256,256]{2,1,0:T(8,128)(2,1)S(1)}, bf16[4,256,256]{2,1,0:T(8,128)(2,1)}, u32[]{:S(2)}) copy-start(bf16[4,256,256]{2,1,0:T(8,128)(2,1)} %param.16) | copy-start | bytes 1572868
  71.8 5.0 %copy-start.25 = (s32[4]{0:T(128)S(1)}, s32[4]{0:T(128)}, u32[]{:S(2)}) copy-start(s32[4]{0:T(128)} %param.19) | copy-start | bytes 52
  76.8 3.8 copy-start.28
  80.2 78.5 %copy-start.5 = (pred[1024,288]{0,1:T(8,128)(4,1)}, pred[1024,288]{0,1:T(8,128)(4,1)S(1)}, u32[]{:S(2)}) copy-start(pred[1024,288]{0,1:T(8,128)(4,1)S(1)} %pad_add_fusion) | copy-start | bytes 884740
  80.4 74.8 %copy-start.6 = (pred[1024,288]{0,1:T(8,128)(4,1)}, pred[1024,288]{0,1:T(8,128)(4,1)S(1)}, u32[]{:S(2)}) copy-start(pred[1024,288]{0,1:T(8,128)(4,1)S(1)} %pad_add_fusion.2) | copy-start | bytes 884740
  83.5 0.6 copy-start.16
  151.3 3.3 copy-start.9
  151.3 3.3 copy-start.12
  153.1 1.5 copy-start.3
  154.6 2.1 copy-start.8
  154.6 2.1 copy-start.13
  155.2 1.4 copy-start.2
  156.6 1.2 copy-start.7
  157.2 1.4 copy-start.1
  158.7 1.4 copy-start.4
  160.7 5.3 %copy-start.18 = (bf16[256,2,128]{2,0,1:T(8,128)(2,1)S(1)}, bf16[256,2,128]{2,0,1:T(8,128)(2,1)}, u32[]{:S(2)}) copy-start(bf16[256,2,128]{2,0,1:T(8,128)(2,1)} %copy.114) | copy-start | bytes 393220
  160.7 5.3 %copy-start.23 = (bf16[32,2,128]{2,0,1:T(8,128)(2,1)S(1)}, bf16[32,2,128]{2,0,1:T(8,128)(2,1)}, u32[]{:S(2)}) copy-start(bf16[32,2,128]{2,0,1:T(8,128)(2,1)} %get-tuple-element.27) | copy-start | bytes 49156
  169.4 3.4 copy-start.22
  176.4 3.4 copy-start.21
  183.3 3.4 copy-start.20
  196.2 0.8 copy-start.15
  207.9 5.9 %copy-start.26 = (s32[4]{0:T(128)S(1)}, s32[4]{0:T(128)}, u32[]{:S(2)}) copy-start(s32[4]{0:T(128)} %param.19) | copy-start | bytes 52
  207.9 5.9 %copy-start.29 = (s32[32]{0:T(128)S(1)}, s32[32]{0:T(128)}, u32[]{:S(2)}) copy-start(s32[32]{0:T(128)} %copy-done.28) | copy-start | bytes 388
  207.9 102.4 %all-to-all-start = ((f32[32,1,33280]{2,1,0:T(1,128)}), f32[32,1,33280]{2,1,0:T(1,128)}, u32[]{:S(2)}, u32[]{:S(2)}) async-start(f32[32,1,33280]{2,1,0:T(1,128)} %copy.137), calls=%async_computation | async-start | bytes 8519680 | tf_op jit(solution)/shard_map/all_to_all | solution.py:122
  213.8 179.3 %reduce-scatter.2.cloned.1.call-start = ((), (), s32[]{:S(2)}) async-start(), calls=%async_computation.4 | async-start | bytes 2359296 | tf_op jit(solution)/shard_map/reduce_scatter | solution.py:143
  336.0 1.9 copy-start.17
Sparse Core Ops, SparseCore 0:
  9.8 45.7 all-gather.2
  62.1 78.0 all-gather.4
  338.0 54.9 reduce-scatter.1

commit v3 on v0

v3 whole, which is shorter than its diff:
```python
import jax
import jax.numpy as jnp
from jax import lax
from jax.sharding import PartitionSpec as P

HD = 128


def rotate(vector, position):
    half_dim = vector.shape[-1] // 2
    frequency = 1000000.0 ** (-(jnp.arange(half_dim, dtype=jnp.float32) * 2.0 / vector.shape[-1]))
    angles = position.astype(jnp.float32)[..., None] * frequency
    cosine = jnp.concatenate([jnp.cos(angles), jnp.cos(angles)], -1)[..., None, :]
    sine = jnp.concatenate([jnp.sin(angles), jnp.sin(angles)], -1)[..., None, :]
    turned = jnp.concatenate([-vector[..., half_dim:], vector[..., :half_dim]], -1)
    return vector * cosine + turned * sine


def body(
    tokens,
    norm_gain,
    w_query,
    w_key,
    w_value,
    w_out,
    cache_keys,
    cache_values,
    cache_len,
    group_len,
):
    seq_index = lax.axis_index("seq")
    seq_count = lax.axis_size("seq")
    requests, local_rows, width_part = tokens.shape
    heads_width = w_query.shape[1]
    local_heads = heads_width // HD
    cache_slots = cache_keys.shape[1]
    gain = norm_gain.astype(jnp.float32)
    offsets = jnp.arange(local_rows, dtype=jnp.int32)
    token_index = seq_index * local_rows + offsets
    slot_index = seq_index * cache_slots + jnp.arange(cache_slots, dtype=jnp.int32)
    query_index = jnp.arange(seq_count * local_rows, dtype=jnp.int32)
    score_scale = HD ** (-0.5)
    numer_width = local_rows * heads_width
    mixed_list = []
    key_list = []
    value_list = []
    for request in range(requests):
        gathered = lax.all_gather(tokens[request], "tensor", axis=1, tiled=True).astype(
            jnp.float32
        )
        inverse_rms = lax.rsqrt(jnp.mean(gathered * gathered, -1, keepdims=True) + 1e-05)
        normed = (gathered * inverse_rms * gain).astype(jnp.bfloat16)

        def project(weight):
            return jnp.dot(normed, weight, preferred_element_type=jnp.float32).reshape(
                local_rows, local_heads, HD
            )

        position = cache_len[request] + token_index
        queries = rotate(project(w_query)[None], position[None])[0].astype(jnp.bfloat16)
        key_new = rotate(project(w_key)[None], position[None])[0].astype(jnp.bfloat16)
        value_new = project(w_value).astype(jnp.bfloat16)
        live_rows = token_index < group_len[request]
        key_list.append(
            jnp.where(live_rows[:, None], key_new.reshape(local_rows, heads_width), 0.0).astype(
                jnp.bfloat16
            )
        )
        value_list.append(
            jnp.where(live_rows[:, None], value_new.reshape(local_rows, heads_width), 0.0).astype(
                jnp.bfloat16
            )
        )
        all_queries = lax.all_gather(queries, "seq", axis=0, tiled=True)
        cache_k = cache_keys[request].reshape(cache_slots, local_heads, HD)
        cache_v = cache_values[request].reshape(cache_slots, local_heads, HD)
        cache_ok = (slot_index < cache_len[request])[None, None, :]
        group_ok = ((token_index[None, :] <= query_index[:, None]) & live_rows[None, :])[None]
        cache_scores = jnp.where(
            cache_ok,
            jnp.einsum("qhd,khd->hqk", all_queries, cache_k, preferred_element_type=jnp.float32)
            * score_scale,
            -1e30,
        )
        group_scores = jnp.where(
            group_ok,
            jnp.einsum("qhd,khd->hqk", all_queries, key_new, preferred_element_type=jnp.float32)
            * score_scale,
            -1e30,
        )
        row_peak = jnp.maximum(jnp.max(cache_scores, -1), jnp.max(group_scores, -1))
        cache_weights = jnp.where(cache_ok, jnp.exp(cache_scores - row_peak[..., None]), 0.0)
        group_weights = jnp.where(group_ok, jnp.exp(group_scores - row_peak[..., None]), 0.0)
        row_mass = jnp.sum(cache_weights, -1) + jnp.sum(group_weights, -1)
        numerators = jnp.einsum(
            "hqk,khd->qhd",
            cache_weights.astype(jnp.bfloat16),
            cache_v,
            preferred_element_type=jnp.float32,
        ) + jnp.einsum(
            "hqk,khd->qhd",
            group_weights.astype(jnp.bfloat16),
            value_new,
            preferred_element_type=jnp.float32,
        )
        stats = jnp.stack([row_peak.T, row_mass.T], -1)
        payload = jnp.concatenate(
            [
                numerators.reshape(seq_count, numer_width),
                stats.reshape(seq_count, local_rows * local_heads * 2),
            ],
            -1,
        )
        received = lax.all_to_all(payload, "seq", 0, 0, tiled=True)
        block_numer = received[:, :numer_width].reshape(seq_count, local_rows, local_heads, HD)
        block_stats = received[:, numer_width:].reshape(seq_count, local_rows, local_heads, 2)
        block_peak = block_stats[..., 0]
        factor = jnp.exp(block_peak - jnp.max(block_peak, 0))
        numer_sum = jnp.sum(block_numer * factor[..., None], 0)
        mass_sum = jnp.sum(block_stats[..., 1] * factor, 0)
        attended = numer_sum / mass_sum[..., None]
        attended = (
            jnp.where(live_rows[:, None, None], attended, 0.0)
            .astype(jnp.bfloat16)
            .reshape(local_rows, heads_width)
        )
        partial_out = jnp.dot(attended, w_out, preferred_element_type=jnp.float32)
        mixed_list.append(
            lax.psum_scatter(partial_out, "tensor", scatter_dimension=1, tiled=True).astype(
                jnp.bfloat16
            )
        )
    return (jnp.stack(mixed_list), jnp.stack(key_list), jnp.stack(value_list))


def solution(mesh):
    placed = (
        P(None, "seq", "tensor"),
        P(),
        P(None, "tensor"),
        P(None, "tensor"),
        P(None, "tensor"),
        P("tensor", None),
        P(None, "seq", "tensor"),
        P(None, "seq", "tensor"),
        P(),
        P(),
    )
    return jax.shard_map(
        body,
        mesh=mesh,
        in_specs=placed,
        out_specs=(P(None, "seq", "tensor"), P(None, "seq", "tensor"), P(None, "seq", "tensor")),
        check_vma=False,
    )
```

time: 645 us -> 637 us (0.988); the launches traced: 642 us -> 627 us
  waiting for transfers between devices: 382 us -> 146 us
  blocking collectives: 126 us -> 278 us
  other arithmetic: 25.6 us -> 58.1 us
  starting transfers between devices: 0.38 us -> 23.8 us
    all_gather x0 -> x8, blocking collectives: none -> 278 us  [the longest x4 162 us: body(): all_queries = lax.all_gather(queries, 'seq', axis=0, tiled=True)]
    pmax x1 -> x0, blocking collectives: 126 us -> none  [body(): lax.pmax(row_peaks.astype(jnp.bfloat16), 'seq').astype(row_peaks.dtype)]
    unnamed x6 -> x4, waiting for transfers between devices: 110 us -> 0.07 us
    all_gather x2 -> x0, waiting for transfers between devices: 88.8 us -> none  [the longest x1 50.7 us: body(): all_queries = lax.all_gather(queries, 'seq', axis=1, tiled=True)]
    reduce_scatter x2 -> x4, waiting for transfers between devices: 183 us -> 106 us  [body(): lax.psum_scatter(partial_out, 'tensor', scatter_dimension=1, tiled=True)]
    all_to_all x0 -> x4, waiting for transfers between devices: none -> 40 us  [body(): received = lax.all_to_all(payload, 'seq', 0, 0, tiled=True)]
    all_to_all x0 -> x8, local copies, waits for them, and re-layouts: none -> 28.6 us  [body(): received = lax.all_to_all(payload, 'seq', 0, 0, tiled=True)]
    all_to_all x0 -> x4, starting transfers between devices: none -> 23.5 us  [body(): received = lax.all_to_all(payload, 'seq', 0, 0, tiled=True)]
  transfers between devices with their start and end apart: 5 -> 8, of which waited for: 5 -> 6; matrix products, arithmetic and copies ran while one was open for 7% -> 19% of each run, Pallas kernels for 0% -> 0%
where the time goes in v3:
time: 637 us; the launch traced here: 627 us
  blocking collectives  278 us (44%)
  waiting for transfers between devices  146 us (23%)
  local copies, waits for them, and re-layouts  72.8 us (11%)
  other arithmetic  58.1 us (9%)
  matrix products  32 us (5%)
  starting transfers between devices  23.8 us (4%)
  between operations  15.5 us (2%)
    all_gather x4, blocking collectives, body(): all_queries = lax.all_gather(queries, 'seq', axis=0, tiled=True)  162 us
    all_gather x4, blocking collectives, body(): lax.all_gather(tokens[request], 'tensor', axis=1, tiled=True)  117 us
    reduce_scatter x4, waiting for transfers between devices, body(): lax.psum_scatter(partial_out, 'tensor', scatter_dimension=1, tiled=True)  106 us
    all_to_all x4, waiting for transfers between devices, body(): received = lax.all_to_all(payload, 'seq', 0, 0, tiled=True)  40 us
    all_to_all x8, local copies, waits for them, and re-layouts, body(): received = lax.all_to_all(payload, 'seq', 0, 0, tiled=True)  28.6 us
    all_to_all x4, starting transfers between devices, body(): received = lax.all_to_all(payload, 'seq', 0, 0, tiled=True)  23.5 us
    dot_general x12, matrix products, project(): jnp.dot(normed, weight, preferred_element_type=jnp.float32)  14.1 us
    reduce_sum x4, other arithmetic, body(): numer_sum = jnp.sum(block_numer * factor[..., None], 0)  13.4 us
  transfers between devices with their start and end apart: 8, of which 6 were waited for; matrix products, arithmetic and copies ran while one was open for 19% of the time, Pallas kernels for 0%

profile of v3, /device:TPU:32, one launch (start us, length us, event | category | flops | bytes accessed | tf_op | source)
XLA Modules:
  0.0 626.5 jit_solution(12570984559530962175)
XLA Ops:
  7.2 1.5 fusion.236
  9.2 1.3 add_convert_fusion
  10.6 1.3 add_convert_fusion.2
  13.7 1.4 fusion.222
  15.1 29.1 %all-gather = bf16[1,32,4096]{2,1,0:T(8,128)(2,1)S(1)} all-gather(bf16[1,32,512]{2,1,0:T(8,128)(2,1)S(1)} %get-tuple-element.11), channel_id=2, replica_groups=mesh['seq'=32,'tensor'=8] {'tensor'}, dimensions={2}, use_global_device_ids=true | all-gather | bytes 294912 | tf_op jit(solution)/shard_map/all_gather | solution.py:48
  44.4 2.1 fusion.216
  46.6 2.1 fusion.218
  49.6 41.5 %all_gather.25 = bf16[1024,2,128]{2,0,1:T(8,128)(2,1)S(1)} all-gather(bf16[32,2,128]{2,0,1:T(8,128)(2,1)S(1)} %get-tuple-element.44), channel_id=1, replica_groups=mesh['seq'=32,'tensor'=8] {'seq'}, dimensions={0}, use_global_device_ids=true | all-gather | bytes 540672 | tf_op jit(solution)/shard_map/all_gather | solution.py:74
  91.2 1.5 fusion.235
  94.9 1.2 broadcast_compare_fusion.2
  100.3 1.8 fusion.220
  109.9 1.8 copy.232
  111.7 2.1 reshape.925
  113.8 1.3 copy.233
  115.1 2.5 reshape.926
  117.6 2.1 copy.234
  119.7 8.9 %all-to-all-start = ((f32[32,1,8320]{2,1,0:T(1,128)}), f32[32,1,8320]{2,1,0:T(1,128)}, u32[]{:S(2)}, u32[]{:S(2)}) async-start(f32[32,1,8320]{2,1,0:T(1,128)} %copy.234), calls=%async_computation | async-start | bytes 2129920 | tf_op jit(solution)/shard_map/all_to_all | solution.py:114
  128.7 29.8 %all-gather.1 = bf16[1,32,4096]{2,1,0:T(8,128)(2,1)S(1)} all-gather(bf16[1,32,512]{2,1,0:T(8,128)(2,1)S(1)} %copy-done.49), channel_id=3, replica_groups=mesh['seq'=32,'tensor'=8] {'tensor'}, dimensions={2}, use_global_device_ids=true | all-gather | bytes 294912 | tf_op jit(solution)/shard_map/all_gather | solution.py:48
  158.7 2.2 fusion.211
  161.5 1.3 fusion.170
  163.9 29.0 %all-gather.2 = bf16[1,32,4096]{2,1,0:T(8,128)(2,1)S(1)} all-gather(bf16[1,32,512]{2,1,0:T(8,128)(2,1)S(1)} %copy-done.48), channel_id=4, replica_groups=mesh['seq'=32,'tensor'=8] {'tensor'}, dimensions={2}, use_global_device_ids=true | all-gather | bytes 294912 | tf_op jit(solution)/shard_map/all_gather | solution.py:48
  197.6 28.7 %all-gather.3 = bf16[1,32,4096]{2,1,0:T(8,128)(2,1)S(1)} all-gather(bf16[1,32,512]{2,1,0:T(8,128)(2,1)S(1)} %copy-done.47), channel_id=5, replica_groups=mesh['seq'=32,'tensor'=8] {'tensor'}, dimensions={2}, use_global_device_ids=true | all-gather | bytes 294912 | tf_op jit(solution)/shard_map/all_gather | solution.py:48
  229.3 39.5 %all_gather.27 = bf16[1024,2,128]{2,0,1:T(8,128)(2,1)S(1)} all-gather(bf16[32,2,128]{2,0,1:T(8,128)(2,1)S(1)} %get-tuple-element.46), channel_id=1, replica_groups=mesh['seq'=32,'tensor'=8] {'seq'}, dimensions={0}, use_global_device_ids=true | all-gather | bytes 540672 | tf_op jit(solution)/shard_map/all_gather | solution.py:74
  275.2 1.8 copy.251
  277.0 2.1 reshape.928
  279.8 1.3 pad_maximum_fusion.4
  281.1 2.0 copy.252
  283.0 3.1 reshape.929
  287.0 2.1 copy.253
  290.2 42.6 %all_gather.29 = bf16[1024,2,128]{2,0,1:T(8,128)(2,1)S(1)} all-gather(bf16[32,2,128]{2,0,1:T(8,128)(2,1)S(1)} %get-tuple-element.48), channel_id=1, replica_groups=mesh['seq'=32,'tensor'=8] {'seq'}, dimensions={0}, use_global_device_ids=true | all-gather | bytes 540672 | tf_op jit(solution)/shard_map/all_gather | solution.py:74
  336.0 1.8 fusion.12
  340.6 1.8 reshape.931
  343.1 1.3 pad_maximum_fusion.5
  344.4 1.2 copy.271
  345.6 1.9 reshape.932
  350.3 38.1 %all_gather.31 = bf16[1024,2,128]{2,0,1:T(8,128)(2,1)S(1)} all-gather(bf16[32,2,128]{2,0,1:T(8,128)(2,1)S(1)} %get-tuple-element.50), channel_id=1, replica_groups=mesh['seq'=32,'tensor'=8] {'seq'}, dimensions={0}, use_global_device_ids=true | all-gather | bytes 540672 | tf_op jit(solution)/shard_map/all_gather | solution.py:74
  388.4 2.3 maximum_bitcast_fusion.2
  390.7 6.4 %all-to-all-start.1 = ((f32[32,1,8320]{2,1,0:T(1,128)}), f32[32,1,8320]{2,1,0:T(1,128)}, u32[]{:S(2)}, u32[]{:S(2)}) async-start(f32[32,1,8320]{2,1,0:T(1,128)} %copy.253), calls=%async_computation.2 | async-start | bytes 2129920 | tf_op jit(solution)/shard_map/all_to_all | solution.py:114
  397.4 3.4 copy.272
  406.1 1.8 reshape.934
  408.1 2.2 fusion.14
  410.9 1.3 reshape.935
  412.1 15.7 %all-to-all-done.1 = f32[32,1,8320]{2,1,0:T(1,128)} async-done(((f32[32,1,8320]{2,1,0:T(1,128)}), f32[32,1,8320]{2,1,0:T(1,128)}, u32[]{:S(2)}, u32[]{:S(2)}) %all-to-all-start.1) | async-done | bytes 1064992 | tf_op jit(solution)/shard_map/all_to_all | solution.py:114
  427.9 3.7 all-to-all-start.2
  431.7 1.3 maximum_bitcast_fusion.3
  433.0 2.1 copy.291
  435.0 5.1 copy.235
  441.3 3.3 fusion.3
  445.0 1.4 fusion.132
  446.5 5.1 copy.254
  452.4 9.9 %all-to-all-done.2 = f32[32,1,8320]{2,1,0:T(1,128)S(1)} async-done(((f32[32,1,8320]{2,1,0:T(1,128)}), f32[32,1,8320]{2,1,0:T(1,128)S(1)}, u32[]{:S(2)}, u32[]{:S(2)}) %all-to-all-start.2) | async-done | bytes 1064992 | tf_op jit(solution)/shard_map/all_to_all | solution.py:114
  462.3 4.5 all-to-all-start.3
  467.3 3.3 fusion.2
  471.0 1.3 fusion.134
  472.6 3.7 copy.273
  477.5 3.3 fusion.1
  481.2 1.3 fusion.136
  482.7 14.4 %all-to-all-done.3 = f32[32,1,8320]{2,1,0:T(1,128)} async-done(((f32[32,1,8320]{2,1,0:T(1,128)}), f32[32,1,8320]{2,1,0:T(1,128)}, u32[]{:S(2)}, u32[]{:S(2)}) %all-to-all-start.3) | async-done | bytes 1064992 | tf_op jit(solution)/shard_map/all_to_all | solution.py:114
  497.1 5.1 copy.292
  503.4 3.4 fusion
  507.1 1.3 fusion.138
  510.7 22.8 %reduce-scatter.7.cloned.1.call-done = f32[32,512]{1,0:T(8,128)} async-done(((f32[32,4096]{1,0:T(8,128)}), f32[32,512]{1,0:T(8,128)}) %reduce-scatter.7.cloned.1.call-update) | async-done | bytes 65552 | tf_op jit(solution)/shard_map/reduce_scatter | solution.py:129
  534.4 41.6 %reduce-scatter.9.cloned.1.call-done = f32[32,512]{1,0:T(8,128)} async-done(((f32[32,4096]{1,0:T(8,128)}), f32[32,512]{1,0:T(8,128)}) %reduce-scatter.9.cloned.1.call-update) | async-done | bytes 65552 | tf_op jit(solution)/shard_map/reduce_scatter | solution.py:129
  576.8 41.5 %reduce-scatter.11.cloned.1.call-done = f32[32,512]{1,0:T(8,128)} async-done(((f32[32,4096]{1,0:T(8,128)}), f32[32,512]{1,0:T(8,128)}) %reduce-scatter.11.cloned.1.call-update) | async-done | bytes 65552 | tf_op jit(solution)/shard_map/reduce_scatter | solution.py:129
  (293 shorter events, 63.4 us)
Async XLA Ops:
  7.2 437.8 %copy-start = (bf16[256,4096]{1,0:T(8,128)(2,1)S(1)}, bf16[256,4096]{1,0:T(8,128)(2,1)}, u32[]{:S(2)}) copy-start(bf16[256,4096]{1,0:T(8,128)(2,1)} %param.15) | copy-start | bytes 6291460
  12.9 36.0 %copy-start.21 = (f32[32,128]{1,0:T(8,128)}, f32[32,128]{1,0:T(8,128)S(1)}, u32[]{:S(2)}) copy-start(f32[32,128]{1,0:T(8,128)S(1)} %maximum_bitcast_fusion.4) | copy-start | bytes 49156
  12.9 36.0 %copy-start.37 = (f32[32,128]{1,0:T(8,128)}, f32[32,128]{1,0:T(8,128)S(1)}, u32[]{:S(2)}) copy-start(f32[32,128]{1,0:T(8,128)S(1)} %maximum_bitcast_fusion.5) | copy-start | bytes 49156
  44.3 2.2 copy-start.60
  46.4 52.0 %copy-start.11 = (bf16[4,256,256]{2,1,0:T(8,128)(2,1)S(1)}, bf16[4,256,256]{2,1,0:T(8,128)(2,1)}, u32[]{:S(2)}) copy-start(bf16[4,256,256]{2,1,0:T(8,128)(2,1)} %param.16) | copy-start | bytes 1572868
  48.9 53.3 %copy-start.19 = (f32[32,2,64]{2,0,1:T(8,128)}, f32[32,2,64]{2,0,1:T(8,128)S(1)}, u32[]{:S(2)}) copy-start(f32[32,2,64]{2,0,1:T(8,128)S(1)} %get-tuple-element.118) | copy-start | bytes 49156
  104.8 2.5 copy-start.40
  104.8 2.5 copy-start.64
  109.4 2.3 copy-start.35
  117.6 11.0 %copy-start.49 = (bf16[1,32,512]{2,1,0:T(8,128)(2,1)S(1)}, bf16[1,32,512]{2,1,0:T(8,128)(2,1)}, u32[]{:S(2)}) copy-start(bf16[1,32,512]{2,1,0:T(8,128)(2,1)} %get-tuple-element.12) | copy-start | bytes 98308
  119.7 270.9 %all-to-all-start = ((f32[32,1,8320]{2,1,0:T(1,128)}), f32[32,1,8320]{2,1,0:T(1,128)}, u32[]{:S(2)}, u32[]{:S(2)}) async-start(f32[32,1,8320]{2,1,0:T(1,128)} %copy.234), calls=%async_computation | async-start | bytes 2129920 | tf_op jit(solution)/shard_map/all_to_all | solution.py:114
  128.6 32.3 %copy-start.2 = (bf16[4096,256]{1,0:T(8,128)(2,1)S(1)}, bf16[4096,256]{1,0:T(8,128)(2,1)}, u32[]{:S(2)}) copy-start(bf16[4096,256]{1,0:T(8,128)(2,1)} %param.12) | copy-start | bytes 6291460
  158.7 4.1 copy-start.4
  160.9 108.8 %copy-start.9 = (f32[32,256]{1,0:T(8,128)}, f32[32,256]{1,0:T(8,128)S(1)}, u32[]{:S(2)}) copy-start(f32[32,256]{1,0:T(8,128)S(1)} %fusion.211) | copy-start | bytes 98308
  160.9 2.9 copy-start.48
  160.9 32.1 %copy-start.1 = (bf16[4096,256]{1,0:T(8,128)(2,1)S(1)}, bf16[4096,256]{1,0:T(8,128)(2,1)}, u32[]{:S(2)}) copy-start(bf16[4096,256]{1,0:T(8,128)(2,1)} %param.13) | copy-start | bytes 6291460
  194.2 3.4 copy-start.47
  226.5 1.8 copy-start.52
  227.0 41.9 %copy-start.15 = (bf16[1,256,256]{2,1,0:T(8,128)(2,1)S(1)}, bf16[1,256,256]{2,1,0:T(8,128)(2,1)}, u32[]{:S(2)}) copy-start(bf16[1,256,256]{2,1,0:T(8,128)(2,1)} %get-tuple-element.9) | copy-start | bytes 393220
  227.0 42.0 %copy-start.16 = (bf16[1,256,256]{2,1,0:T(8,128)(2,1)S(1)}, bf16[1,256,256]{2,1,0:T(8,128)(2,1)}, u32[]{:S(2)}) copy-start(bf16[1,256,256]{2,1,0:T(8,128)(2,1)} %get-tuple-element.5) | copy-start | bytes 393220
  228.2 40.6 %copy-start.23 = (f32[32,128]{1,0:T(8,128)}, f32[32,128]{1,0:T(8,128)S(1)}, u32[]{:S(2)}) copy-start(f32[32,128]{1,0:T(8,128)S(1)} %maximum_bitcast_fusion.6) | copy-start | bytes 49156
  228.3 40.5 %copy-start.38 = (f32[32,128]{1,0:T(8,128)}, f32[32,128]{1,0:T(8,128)S(1)}, u32[]{:S(2)}) copy-start(f32[32,128]{1,0:T(8,128)S(1)} %maximum_bitcast_fusion.7) | copy-start | bytes 49156
  228.6 40.3 %copy-start.20 = (f32[32,2,64]{2,0,1:T(8,128)}, f32[32,2,64]{2,0,1:T(8,128)S(1)}, u32[]{:S(2)}) copy-start(f32[32,2,64]{2,0,1:T(8,128)S(1)} %get-tuple-element.114) | copy-start | bytes 49156
  268.8 3.2 copy-start.63
  270.9 2.4 copy-start.41
  272.0 2.8 copy-start.29
  286.1 2.9 copy-start.51
  286.1 3.0 copy-start.50
  286.9 2.3 copy-start.7
  286.9 2.4 copy-start.18
  286.9 45.9 %copy-start.13 = (bf16[1,256,256]{2,1,0:T(8,128)(2,1)S(1)}, bf16[1,256,256]{2,1,0:T(8,128)(2,1)}, u32[]{:S(2)}) copy-start(bf16[1,256,256]{2,1,0:T(8,128)(2,1)} %get-tuple-element.8) | copy-start | bytes 393220
  286.9 46.0 %copy-start.14 = (bf16[1,256,256]{2,1,0:T(8,128)(2,1)S(1)}, bf16[1,256,256]{2,1,0:T(8,128)(2,1)}, u32[]{:S(2)}) copy-start(bf16[1,256,256]{2,1,0:T(8,128)(2,1)} %get-tuple-element.4) | copy-start | bytes 393220
  289.1 43.7 %copy-start.25 = (f32[32,128]{1,0:T(8,128)}, f32[32,128]{1,0:T(8,128)S(1)}, u32[]{:S(2)}) copy-start(f32[32,128]{1,0:T(8,128)S(1)} %maximum_bitcast_fusion.8) | copy-start | bytes 49156
  289.2 43.6 %copy-start.39 = (f32[32,128]{1,0:T(8,128)}, f32[32,128]{1,0:T(8,128)S(1)}, u32[]{:S(2)}) copy-start(f32[32,128]{1,0:T(8,128)S(1)} %maximum_bitcast_fusion.9) | copy-start | bytes 49156
  334.8 3.1 copy-start.42
  334.8 3.0 copy-start.62
  336.0 3.4 copy-start.30
  340.6 8.0 %copy-start.17 = (f32[32,256]{1,0:T(8,128)S(1)}, f32[32,256]{1,0:T(8,128)}, u32[]{:S(2)}) copy-start(f32[32,256]{1,0:T(8,128)} %fusion.203) | copy-start | bytes 98308
  348.4 48.7 %copy-start.27 = (f32[32,128]{1,0:T(8,128)}, f32[32,128]{1,0:T(8,128)S(1)}, u32[]{:S(2)}) copy-start(f32[32,128]{1,0:T(8,128)S(1)} %maximum_bitcast_fusion.10) | copy-start | bytes 49156
  390.7 10.2 %copy-start.12 = (bf16[1,256,256]{2,1,0:T(8,128)(2,1)S(1)}, bf16[1,256,256]{2,1,0:T(8,128)(2,1)}, u32[]{:S(2)}) copy-start(bf16[1,256,256]{2,1,0:T(8,128)(2,1)} %get-tuple-element.10) | copy-start | bytes 393220
  390.7 37.2 %all-to-all-start.1 = ((f32[32,1,8320]{2,1,0:T(1,128)}), f32[32,1,8320]{2,1,0:T(1,128)}, u32[]{:S(2)}, u32[]{:S(2)}) async-start(f32[32,1,8320]{2,1,0:T(1,128)} %copy.253), calls=%async_computation.2 | async-start | bytes 2129920 | tf_op jit(solution)/shard_map/all_to_all | solution.py:114
  400.8 2.5 copy-start.59
  405.3 2.7 copy-start.66
  427.9 34.4 %all-to-all-start.2 = ((f32[32,1,8320]{2,1,0:T(1,128)}), f32[32,1,8320]{2,1,0:T(1,128)S(1)}, u32[]{:S(2)}, u32[]{:S(2)}) async-start(f32[32,1,8320]{2,1,0:T(1,128)} %copy.272), calls=%async_computation.4 | async-start | bytes 2129920 | tf_op jit(solution)/shard_map/all_to_all | solution.py:114
  431.6 78.2 %reduce-scatter.5.cloned.1.call-start = ((), (), s32[]{:S(2)}) async-start(), calls=%async_computation.8 | async-start | bytes 589824 | tf_op jit(solution)/shard_map/reduce_scatter | solution.py:129
  441.3 3.7 copy-start.57
  444.6 1.8 copy-start.22
  444.6 1.8 copy-start.36
  444.6 1.8 copy-start.43
  462.3 34.9 %all-to-all-start.3 = ((f32[32,1,8320]{2,1,0:T(1,128)}), f32[32,1,8320]{2,1,0:T(1,128)}, u32[]{:S(2)}, u32[]{:S(2)}) async-start(f32[32,1,8320]{2,1,0:T(1,128)} %copy.291), calls=%async_computation.6 | async-start | bytes 2129920 | tf_op jit(solution)/shard_map/all_to_all | solution.py:114
  466.7 66.8 %reduce-scatter.7.cloned.1.call-start = ((), (), s32[]{:S(2)}) async-start(), calls=%async_computation.9 | async-start | bytes 589824 | tf_op jit(solution)/shard_map/reduce_scatter | solution.py:129
  467.3 3.7 copy-start.56
  470.7 1.8 copy-start.24
  470.7 1.8 copy-start.10
  470.7 1.8 copy-start.34
  470.7 1.8 copy-start.44
  472.4 103.6 %reduce-scatter.9.cloned.1.call-start = ((), (), s32[]{:S(2)}) async-start(), calls=%async_computation.10 | async-start | bytes 589824 | tf_op jit(solution)/shard_map/reduce_scatter | solution.py:129
  477.5 3.7 copy-start.55
  480.8 1.7 copy-start.26
  480.8 1.8 copy-start.8
  480.8 1.8 copy-start.32
  480.8 1.8 copy-start.45
  482.5 135.7 %reduce-scatter.11.cloned.1.call-start = ((), (), s32[]{:S(2)}) async-start(), calls=%async_computation.11 | async-start | bytes 589824 | tf_op jit(solution)/shard_map/reduce_scatter | solution.py:129
  503.4 3.7 copy-start.54
  (11 other events, 17.5 us)
Sparse Core Ops, SparseCore 0:
  446.5 43.6 reduce-scatter.4
  492.7 40.7 reduce-scatter.6
  536.0 39.8 reduce-scatter.8
  578.3 39.8 reduce-scatter.10
